TPU v7x, 256 devices: a whole 4x4x8 slice. The times are simulated.
256 devices in a mesh: guide: 2 (over x_hi), req: 128 (over x_lo, y, z, core).
Axes of the slice: x: 4 (x_hi: 2, x_lo: 2; x = x_hi * 2 + x_lo), y: 4, z: 8, core: 2. Of those that a mesh axis runs over, the one named last changes fastest.
Arguments:
- hidden_in: bfloat16 [2, 3072, 2048], P('guide', 'req'), may hold values from -24 to 24
- attn_gain: float32 [2048], replicated, may hold values from 0.25 to 1.75
- w_qkv: bfloat16 [2048, 1920], P('guide'), may hold values from -0.125 to 0.125
- w_out: bfloat16 [1280, 2048], P('guide'), may hold values from -0.3125 to 0.3125
- final_gain: float32 [2048], replicated, may hold values from 0.25 to 1.75
- w_vocab: bfloat16 [2048, 32000], P(None, 'req'), may hold values from -0.125 to 0.125
- kv_pool: bfloat16 [2, 5888, 64, 640], P('guide', 'req'), may hold values from -1400 to 1400
- cache_len: int32 [2, 3072], P('guide'), may hold values from 1 to 512, as said below
- page_table: int32 [2, 3072, 8], P('guide'), may hold values from 0 to 45, as said below
- migrations: int32 [2, 128, 3], P('guide'), may hold values from 0 to 3071, as said below
Outputs:
- guided: float32 [3072, 32000], P('guide', 'req')
Inputs may be any that keep to these rules, and one draw needn't show every extreme that they name: `cache_len`: cached tokens of a request of group 0 number at most 512, of group 1 at most 256; both bounds are reached in each group. `page_table`: row i lists request i's pages in order as numbers within the pool of its owner (old owner if listed, else req index i // 24); entries past its last page are 0; pages of different requests on one device differ. `migrations`: 128 rows per group, distinct requests; the new owner is request // 24; the old owner differs from it by 1 to 2 modulo 128; at most one row per pair of owners; a listed request has at most 2 pages; in each group some new owner receives, from each of its 4 nearest old owners, a request of 2 pages.
All inputs are finite; a program needn't handle non-finite values.
Results may differ from a plain program's by a relative error of at most 0.011.
The roundings to bfloat16 on the way count: a program that leaves them out, or rounds other values in their place, can miss the bound.
Values may be sent and summed in bfloat16 or wider, within the bound.
No kernel may reach another device: no remote copies, remote signals or barrier semaphores. Data moves between devices by JAX's collectives and lax.ppermute only.
A program may use at most 128 MiB of HBM per device.

v0:
```python
import math
import jax
import jax.numpy as jnp
from jax import lax
from jax.sharding import PartitionSpec as P

QH = 20
KVH = 5
HD = 64
MAXP = 8
MIGP = 2
HOP = 2
epsilon = 1e-06
guidance = 3.0


def from_partner(block, axis, bit):
    count = lax.axis_size(axis)
    route = []
    for low in range(count):
        high = low | 1 << bit
        if high != low and high < count:
            route += [(low, high), (high, low)]
    return lax.ppermute(block, axis, route)


def shifted(value, axis, steps):
    count = lax.axis_size(axis)
    pairs = [(source, (source + steps) % count) for source in range(count)]
    return lax.ppermute(value, axis, pairs)


def rms_scale(values, gain):
    return values * lax.rsqrt(jnp.mean(values * values, axis=-1, keepdims=True) + epsilon) * gain


def masked_scores(queries, page_rows, lengths):
    count = page_rows.shape[0]
    span = page_rows.shape[1]
    half_width = page_rows.shape[2] // 2
    key_rows = page_rows[:, :, :half_width].reshape(count, span, KVH, HD)
    value_rows = page_rows[:, :, half_width:].reshape(count, span, KVH, HD)
    scores = jnp.einsum(
        "rkgd,rskd->rkgs", queries, key_rows, preferred_element_type=jnp.float32
    ) * (1.0 / math.sqrt(HD))
    living = jnp.arange(span, dtype=jnp.int32)[None, :] < lengths[:, None]
    scores = jnp.where(living[:, None, None, :], scores, -jnp.inf)
    return (scores, value_rows)


def attend_all(queries, page_rows, lengths, own_score, value_new):
    scores, value_rows = masked_scores(queries, page_rows, lengths)
    highest = jnp.maximum(jnp.max(scores, axis=-1), own_score)
    weights = jnp.exp(scores - highest[..., None])
    own_weight = jnp.exp(own_score - highest)
    denominator = jnp.sum(weights, axis=-1) + own_weight
    weighted = jnp.einsum(
        "rkgs,rskd->rkgd",
        weights.astype(jnp.bfloat16),
        value_rows,
        preferred_element_type=jnp.float32,
    )
    own_rounded = own_weight.astype(jnp.bfloat16).astype(jnp.float32)
    weighted = weighted + own_rounded[..., None] * value_new.astype(jnp.float32)[:, :, None, :]
    return (highest, denominator, weighted)


def gather_pages(pool, tables):
    picked = pool[tables]
    return picked.reshape(tables.shape[0], tables.shape[1] * pool.shape[1], pool.shape[2])


def body(
    hidden_in,
    attn_gain,
    w_qkv,
    w_out,
    final_gain,
    w_vocab,
    kv_pool,
    cache_len,
    page_table,
    migrations,
):
    device = lax.axis_index("req")
    devices = lax.axis_size("req")
    side = lax.axis_index("guide")
    local_rows = hidden_in.shape[1]
    group = QH // KVH
    query_width = QH * HD
    key_width = KVH * HD
    scaling = 1.0 / math.sqrt(HD)
    slots = 2 * HOP
    offsets = [number - HOP if number < HOP else number - HOP + 1 for number in range(slots)]
    states_in = hidden_in[0].astype(jnp.float32)
    normed = rms_scale(states_in, attn_gain).astype(jnp.bfloat16)
    partner_normed = from_partner(normed, "guide", 0)
    both_normed = jnp.where(
        side == 0, jnp.stack([normed, partner_normed]), jnp.stack([partner_normed, normed])
    )
    inner_half = w_qkv.shape[0]
    normed_part = lax.dynamic_slice_in_dim(both_normed, side * inner_half, inner_half, 2)
    selected = normed_part
    joined = lax.psum_scatter(
        jnp.einsum("grd,df->grf", selected, w_qkv, preferred_element_type=jnp.float32),
        "guide",
        scatter_dimension=0,
        tiled=True,
    )[0].astype(jnp.bfloat16)
    queries = joined[:, :query_width].reshape(local_rows, KVH, group, HD)
    new_keys = joined[:, query_width : query_width + key_width].reshape(local_rows, KVH, HD)
    new_values = joined[:, query_width + key_width :].reshape(local_rows, KVH, HD)
    own_score = (
        jnp.einsum("rkgd,rkd->rkg", queries, new_keys, preferred_element_type=jnp.float32) * scaling
    )
    tables = page_table[0]
    lengths_all = cache_len[0]
    listing = migrations[0]
    pool = kv_pool[0]
    pool_pages = pool.shape[0]
    first_row = device * local_rows
    own_table = lax.dynamic_slice_in_dim(tables, first_row, local_rows, 0)
    own_lengths = lax.dynamic_slice_in_dim(lengths_all, first_row, local_rows, 0)
    global_ids = first_row + jnp.arange(local_rows, dtype=jnp.int32)
    matches = listing[None, :, 0] == global_ids[:, None]
    is_moved = jnp.any(matches, axis=1)
    old_owner = jnp.sum(jnp.where(matches, listing[None, :, 1], 0), axis=1)
    distance = jnp.remainder(device - old_owner, devices)
    slot_of = jnp.where(distance <= HOP, HOP + distance - 1, HOP - (devices - distance))
    arrivals = []
    for number in range(slots):
        offset = offsets[number]
        holding = (listing[:, 1] == device) & (
            listing[:, 2] == jnp.remainder(device + offset, devices)
        )
        held_request = listing[jnp.argmax(holding), 0]
        pages_sent = pool[tables[held_request, :MIGP]]
        arrivals.append(shifted(pages_sent, "req", offset))
    extended = jnp.concatenate([pool] + arrivals, axis=0)
    page_column = jnp.minimum(jnp.arange(MAXP, dtype=jnp.int32), MIGP - 1)
    moved_pages = pool_pages + slot_of[:, None] * MIGP + page_column[None, :]
    used_table = jnp.where(is_moved[:, None], moved_pages, own_table)
    tops, sums, accs = attend_all(
        queries, gather_pages(extended, used_table), own_lengths, own_score, new_values
    )
    attended = (accs / sums[..., None]).reshape(local_rows, query_width).astype(jnp.bfloat16)
    partner_attended = from_partner(attended, "guide", 0)
    both_attended = jnp.where(
        side == 0, jnp.stack([attended, partner_attended]), jnp.stack([partner_attended, attended])
    )
    head_half = w_out.shape[0]
    attended_part = lax.dynamic_slice_in_dim(both_attended, side * head_half, head_half, 2)
    selected = attended_part
    state_after = (
        states_in
        + lax.psum_scatter(
            jnp.einsum("grc,cd->grd", selected, w_out, preferred_element_type=jnp.float32).astype(
                jnp.bfloat16
            ),
            "guide",
            scatter_dimension=0,
            tiled=True,
        ).astype(jnp.float32)[0]
    )
    final = rms_scale(state_after, final_gain).astype(jnp.bfloat16)
    logits = jnp.dot(
        lax.all_gather(final, "req", axis=0, tiled=True),
        w_vocab,
        preferred_element_type=jnp.float32,
    )
    halves = logits.reshape(2, logits.shape[0] // 2, logits.shape[1])
    paired = lax.all_to_all(
        halves.astype(jnp.bfloat16), "guide", split_axis=0, concat_axis=0, tiled=True
    ).astype(halves.dtype)
    return paired[1] + guidance * (paired[0] - paired[1])


def solution(mesh):
    in_specs = (
        P("guide", "req", None),
        P(),
        P("guide", None),
        P("guide", None),
        P(),
        P(None, "req"),
        P("guide", "req", None, None),
        P("guide", None),
        P("guide", None, None),
        P("guide", None, None),
    )
    out_specs = P("guide", "req")
    return jax.shard_map(body, mesh=mesh, in_specs=in_specs, out_specs=out_specs, check_vma=False)
```

profile of v0, /device:TPU:32, one launch (start us, length us, event | category | flops | bytes accessed | tf_op | source)
XLA Modules:
  0.0 425.6 jit_solution(11976493014555277146)
XLA Ops:
  6.5 0.8 copy.45
  7.4 0.7 fusion.49
  9.5 0.6 fusion.48
  11.3 0.7 fusion.47
  13.3 0.7 fusion.46
  17.8 1.5 constant_dynamic-slice_fusion.8
  26.8 1.0 fusion.53
  27.9 2.6 gather_fusion
  30.5 1.9 collective-permute-start.1
  32.4 2.7 gather_fusion.1
  35.1 6.8 %collective-permute-start.2 = (bf16[2,64,640]{2,1,0:T(8,128)(2,1)S(1)}, bf16[2,64,640]{2,1,0:T(8,128)(2,1)S(1)}, u32[]{:S(2)}, u32[]{:S(2)}) collective-permute-start(bf16[2,64,640]{2,1,0:T(8,128)(2,1)S(1)} %gather_fusion.1), channel_id=1, source_target_pairs={{0,127},{1,0},{2,1},{3,2},{4,3},{5,4},{6,5},{7,6},{8,7},{9,8},{10,... | collective-permute-start | bytes 491528 | tf_op jit(solution)/shard_map/ppermute | solution.py:30
  41.9 3.3 gather_fusion.2
  45.2 3.3 gather_fusion.3
  48.5 1.0 fusion.20
  49.5 1.6 fusion.22
  51.1 2.7 collective-permute-start
  53.9 4.2 constant_dynamic-update-slice_fusion.4
  58.2 0.2 compare_reduce_fusion
  58.6 0.8 compare_select_fusion.1
  59.6 0.8 fusion.60
  60.4 3.7 fusion
  64.1 0.2 reduce-scatter.5.cloned.1.call-start
  64.4 0.7 constant_dynamic-update-slice_fusion.3
  65.1 0.7 constant_dynamic-update-slice_fusion.2
  65.8 1.6 constant_dynamic-update-slice_fusion.1
  67.4 1.6 constant_dynamic-update-slice_fusion
  69.0 11.3 %gather_fusion.4 = bf16[192,64,640]{2,1,0:T(8,128)(2,1)} fusion(bf16[54,64,640]{2,1,0:T(8,128)(2,1)} %constant_dynamic-update-slice_fusion, s32[1024]{0:T(1024)S(1)} %pad_clamp_fusion), kind=kCustom, calls=%fused_computation.4 | custom fusion | bytes 31458048 | tf_op jit(solution)/shard_map/gather | solution.py:69
  80.3 16.9 %fusion.64 = (bf16[24,512,320]{2,1,0:T(8,128)(2,1)}, bf16[24,512,320]{2,1,0:T(8,128)(2,1)}) fusion(bf16[24,512,640]{2,1,0:T(8,128)(2,1)} %bitcast.139), kind=kLoop, calls=%fused_computation.128 | loop fusion | bytes 31457280 | tf_op jit(solution)/shard_map/slice | solution.py:41
  97.2 11.6 %copy.27 = bf16[24,512,320]{1,2,0:T(8,128)(2,1)} copy(bf16[24,512,320]{2,1,0:T(8,128)(2,1)} %get-tuple-element.17) | data formatting | bytes 15728640
  108.7 11.5 %copy.28 = bf16[24,512,320]{1,2,0:T(8,128)(2,1)} copy(bf16[24,512,320]{2,1,0:T(8,128)(2,1)} %get-tuple-element.18) | data formatting | bytes 15728640
  120.2 0.9 convert_bitcast_fusion.1
  121.5 0.3 fusion.66
  121.8 4.5 %fusion.65 = (f32[24,5,4]{2,1,0:T(8,128)S(1)}, f32[24,5,4,512]{3,2,1,0:T(4,128)S(1)}) fusion(bf16[24,5,4,64]{3,2,1,0:T(4,128)(2,1)S(1)} %reshape.351, bf16[24,512,5,64]{1,3,2,0:T(8,128)(2,1)} %bitcast.140, pred[24,512]{1,0:T(8,128)(4,1)S(1)} %iota_compare_fusion), kind=kOutput, calls=%fused_computation.129 | convolution fusion | flops 32194080 | bytes 8923008 | tf_op jit(solution)/shard_map/rkgd,rskd->rkgs/dot_general | solution.py:43
  126.3 0.9 copy-done.1
  127.2 0.6 fusion.13
  127.9 5.8 %fusion.12 = bf16[24,5,4,64]{3,2,1,0:T(4,128)(2,1)S(1)} fusion(bf16[24,512,5,64]{1,3,2,0:T(8,128)(2,1)} %bitcast.141, f32[24,5,4,512]{3,2,1,0:T(4,128)} %copy-done.1, f32[24,5,4]{2,1,0:T(8,128)S(1)} %fusion.31, f32[24,5,4]{2,1,0:T(8,128)S(1)} %get-tuple-element.20, f32[24,5,64]{2,1,0:T(8,128)S(1)} %reshape.357, f32[24,5,4]{2,1,0:T(8,128)S(1)} %get-tuple-element.19), kind=kOutput, calls=%fused_computation.20 | convolution fusion | flops 32071680 | bytes 8945280 | tf_op jit(solution)/shard_map/rkgs,rskd->rkgd/dot_general | solution.py:57
  133.9 0.8 collective-permute-start.5
  134.8 4.9 %collective-permute-done.5 = bf16[24,1280]{1,0:T(8,128)(2,1)S(1)} collective-permute-done((bf16[24,1280]{1,0:T(8,128)(2,1)S(1)}, bf16[24,1280]{1,0:T(8,128)(2,1)S(1)}, u32[]{:S(2)}, u32[]{:S(2)}) %collective-permute-start.5) | collective-permute-done | bytes 61472 | tf_op jit(solution)/shard_map/ppermute | solution.py:24
  139.7 1.2 fusion.4
  141.0 0.3 all-gather.2.cloned.1.call-start
  141.2 15.0 %reduce-scatter.5.cloned.1.call-done = bf16[1,24,2048]{2,1,0:T(8,128)(2,1)} async-done(((bf16[2,24,2048]{2,1,0:T(8,128)(2,1)}), bf16[1,24,2048]{2,1,0:T(8,128)(2,1)}) %reduce-scatter.5.cloned.1.call-update) | async-done | bytes 98320 | tf_op jit(solution)/shard_map/reduce_scatter | solution.py:156
  156.2 1.0 multiply_reduce_fusion
  157.3 1.6 multiply_convert_fusion
  158.9 225.8 %all-gather.2.cloned.1.call-done = bf16[3072,2048]{1,0:T(8,128)(2,1)} async-done(((bf16[24,2048]{1,0:T(8,128)(2,1)}), bf16[3072,2048]{1,0:T(8,128)(2,1)}) %all-gather.2.cloned.1.call-update) | async-done | bytes 12582928 | tf_op jit(solution)/shard_map/all_gather | solution.py:167
  384.7 8.2 %convolution_convert_fusion = bf16[3072,250]{1,0:T(8,128)(2,1)S(1)} fusion(bf16[3072,2048]{1,0:T(8,128)(2,1)} %all-gather.2.cloned.1.call-done, bf16[2048,250]{1,0:T(8,128)(2,1)} %param.15), kind=kOutput, calls=%fused_computation.7 | convolution fusion | flops 3146496000 | bytes 15142912 | tf_op jit(solution)/shard_map/dot_general | solution.py:166
  392.9 24.5 %all_to_all.5 = bf16[2,1536,250]{2,1,0:T(8,128)(2,1)S(1)} all-to-all(bf16[2,1536,250]{2,1,0:T(8,128)(2,1)S(1)} %bitcast.146), channel_id=1, replica_groups=mesh['guide'=2,'req'=128] {'guide'}, dimensions={0} | all-to-all | bytes 3072000 | tf_op jit(solution)/shard_map/all_to_all | solution.py:172
  417.4 0.2 convert_element_type.91
  417.7 1.3 fusion.9
  (48 shorter events, 1.4 us)
Async XLA Ops:
  6.5 133.2 %copy-start = (bf16[640,2048]{1,0:T(8,128)(2,1)S(1)}, bf16[640,2048]{1,0:T(8,128)(2,1)}, u32[]{:S(2)}) copy-start(bf16[640,2048]{1,0:T(8,128)(2,1)} %param.13) | copy-start | bytes 7864324
  6.5 113.7 %reduce-scatter.7.cloned.1.call-start = ((), (), s32[]{:S(2)}) async-start(), calls=%async_computation.5 | async-start | bytes 552960
  30.5 33.9 %collective-permute-start.1 = (bf16[2,64,640]{2,1,0:T(8,128)(2,1)S(1)}, bf16[2,64,640]{2,1,0:T(8,128)(2,1)S(1)}, u32[]{:S(2)}, u32[]{:S(2)}) collective-permute-start(bf16[2,64,640]{2,1,0:T(8,128)(2,1)S(1)} %gather_fusion), channel_id=1, source_target_pairs={{0,126},{1,127},{2,0},{3,1},{4,2},{5,3},{6,4},{7,5},{8,6},{9,7},{1... | collective-permute-start | bytes 491528 | tf_op jit(solution)/shard_map/ppermute | solution.py:30
  32.4 25.7 %copy-start.2 = (bf16[1,24,2048]{2,1,0:T(8,128)(2,1)S(1)}, bf16[1,24,2048]{2,1,0:T(8,128)(2,1)}, u32[]{:S(2)}) copy-start(bf16[1,24,2048]{2,1,0:T(8,128)(2,1)} %param.10) | copy-start | bytes 294916
  32.4 25.7 %copy-start.3 = (f32[2048]{0:T(1024)S(1)}, f32[2048]{0:T(1024)}, u32[]{:S(2)}) copy-start(f32[2048]{0:T(1024)} %param.11) | copy-start | bytes 24580
  35.1 30.0 %collective-permute-start.2 = (bf16[2,64,640]{2,1,0:T(8,128)(2,1)S(1)}, bf16[2,64,640]{2,1,0:T(8,128)(2,1)S(1)}, u32[]{:S(2)}, u32[]{:S(2)}) collective-permute-start(bf16[2,64,640]{2,1,0:T(8,128)(2,1)S(1)} %gather_fusion.1), channel_id=1, source_target_pairs={{0,127},{1,0},{2,1},{3,2},{4,3},{5,4},{6,5},{7,6},{8,7},{9,8},{10,... | collective-permute-start | bytes 491528 | tf_op jit(solution)/shard_map/ppermute | solution.py:30
  45.2 20.6 %collective-permute-start.3 = (bf16[2,64,640]{2,1,0:T(8,128)(2,1)}, bf16[2,64,640]{2,1,0:T(8,128)(2,1)}, u32[]{:S(2)}, u32[]{:S(2)}) collective-permute-start(bf16[2,64,640]{2,1,0:T(8,128)(2,1)} %gather_fusion.2), channel_id=1, source_target_pairs={{0,1},{1,2},{2,3},{3,4},{4,5},{5,6},{6,7},{7,8},{8,9},{9,10},{10,1... | collective-permute-start | bytes 491528 | tf_op jit(solution)/shard_map/ppermute | solution.py:30
  48.5 18.9 %collective-permute-start.4 = (bf16[2,64,640]{2,1,0:T(8,128)(2,1)}, bf16[2,64,640]{2,1,0:T(8,128)(2,1)}, u32[]{:S(2)}, u32[]{:S(2)}) collective-permute-start(bf16[2,64,640]{2,1,0:T(8,128)(2,1)} %gather_fusion.3), channel_id=1, source_target_pairs={{0,2},{1,3},{2,4},{3,5},{4,6},{5,7},{6,8},{7,9},{8,10},{9,11},{10,... | collective-permute-start | bytes 491528 | tf_op jit(solution)/shard_map/ppermute | solution.py:30
  51.1 9.3 %collective-permute-start = (bf16[24,2048]{1,0:T(8,128)(2,1)}, bf16[24,2048]{1,0:T(8,128)(2,1)}, u32[]{:S(2)}, u32[]{:S(2)}) collective-permute-start(bf16[24,2048]{1,0:T(8,128)(2,1)} %fusion.22), channel_id=1, source_target_pairs={{0,128},{128,0},{1,129},{129,1},{2,130},{130,2},{3,131},{131,3},{4... | collective-permute-start | bytes 294920 | tf_op jit(solution)/shard_map/ppermute | solution.py:24
  64.1 92.1 %reduce-scatter.5.cloned.1.call-start = ((), (), s32[]{:S(2)}) async-start(), calls=%async_computation.3 | async-start | bytes 294912 | tf_op jit(solution)/shard_map/reduce_scatter | solution.py:156
  126.2 0.9 copy-start.1
  133.7 23.5 %copy-start.4 = (f32[2048]{0:T(1024)S(1)}, f32[2048]{0:T(1024)}, u32[]{:S(2)}) copy-start(f32[2048]{0:T(1024)} %param.14) | copy-start | bytes 24580
  133.9 5.8 %collective-permute-start.5 = (bf16[24,1280]{1,0:T(8,128)(2,1)S(1)}, bf16[24,1280]{1,0:T(8,128)(2,1)S(1)}, u32[]{:S(2)}, u32[]{:S(2)}) collective-permute-start(bf16[24,1280]{1,0:T(8,128)(2,1)S(1)} %convert_element_type.86), channel_id=1, source_target_pairs={{0,128},{128,0},{1,129},{129,1},{2,130},{130,2},{3,131},{131,3},{4... | collective-permute-start | bytes 184328 | tf_op jit(solution)/shard_map/ppermute | solution.py:24
  141.0 243.7 %all-gather.2.cloned.1.call-start = ((), (), s32[]{:S(2)}) async-start(), calls=%async_computation.4 | async-start | bytes 12681216 | tf_op jit(solution)/shard_map/all_gather | solution.py:167
Sparse Core Ops, SparseCore 0:
  64.3 17.4 reduce-scatter.6
  141.1 15.0 reduce-scatter.4
  159.0 225.6 all-gather.1
where the time goes:
time: 427 us; the launch traced here: 426 us
  waiting for transfers between devices  246 us (58%)
  local copies, waits for them, and re-layouts  77.8 us (18%)
  between operations  28.5 us (7%)
  blocking collectives  24.5 us (6%)
  matrix products  23.7 us (6%)
  other arithmetic  12.8 us (3%)
  starting transfers between devices  12.6 us (3%)
    all_gather x1, waiting for transfers between devices, body(): lax.all_gather(final, 'req', axis=0, tiled=True)  226 us
    unnamed x17, local copies, waits for them, and re-layouts  32.1 us
    all_to_all x1, blocking collectives, body(): lax.all_to_all(halves.astype(jnp.bfloat16), 'guide', split_axis=0, concat...  24.5 us
    slice x1, local copies, waits for them, and re-layouts, masked_scores(): key_rows = page_rows[:, :, :half_width].reshape(count, span, KVH, HD)  16.9 us
    reduce_scatter x1, waiting for transfers between devices, body(): lax.psum_scatter(jnp.einsum('grc,cd->grd', selected, w_out, preferred_ele...  15 us
    gather x4, local copies, waits for them, and re-layouts, body(): pages_sent = pool[tables[held_request, :MIGP]]  11.9 us
    gather x1, local copies, waits for them, and re-layouts, gather_pages(): picked = pool[tables]  11.3 us
    ppermute x4, starting transfers between devices, shifted(): return lax.ppermute(value, axis, pairs)  8.66 us
  transfers between devices with their start and end apart: 9, of which 3 were waited for; matrix products, arithmetic and copies ran while one was open for 18% of the time, Pallas kernels for 0%

commit v1 on v0

--- a/solution.py
+++ b/solution.py
@@ -164,7 +164,9 @@
     )
     final = rms_scale(state_after, final_gain).astype(jnp.bfloat16)
     logits = jnp.dot(
-        lax.all_gather(final, "req", axis=0, tiled=True),
+        jnp.concatenate(
+            lax.all_to_all(jnp.stack([final] * lax.axis_size("req")), "req", 0, 0), axis=0
+        ),
         w_vocab,
         preferred_element_type=jnp.float32,
     )

time: 427 us -> 490 us (1.15)
  blocking collectives: 24.5 us -> 312 us
  waiting for transfers between devices: 246 us -> 20.2 us
  local copies, waits for them, and re-layouts: 77.8 us -> 83.9 us
    all_to_all x0 -> x1, blocking collectives: none -> 288 us  [body(): lax.all_to_all(jnp.stack([final] * lax.axis_size('req')), 'req', 0, 0)]
    all_gather x1 -> x0, waiting for transfers between devices: 226 us -> none  [body(): lax.all_gather(final, 'req', axis=0, tiled=True)]
    another operation x0 -> x1, local copies, waits for them, and re-layouts: none -> 6.17 us  [body(): jnp.stack([final] * lax.axis_size('req'))]
    unnamed x17 -> x19, local copies, waits for them, and re-layouts: 32.1 us -> 32.1 us
  transfers between devices with their start and end apart: 9 -> 8, of which waited for: 3 -> 2; matrix products, arithmetic and copies ran while one was open for 18% -> 16% of each run, Pallas kernels for 0% -> 0%
where the time goes in v1:
time: 490 us; the launch traced here: 488 us
  blocking collectives  312 us (64%)
  local copies, waits for them, and re-layouts  83.9 us (17%)
  between operations  28.8 us (6%)
  waiting for transfers between devices  20.2 us (4%)
  matrix products  19 us (4%)
  starting transfers between devices  12.4 us (3%)
  other arithmetic  12.1 us (2%)
    all_to_all x1, blocking collectives, body(): lax.all_to_all(jnp.stack([final] * lax.axis_size('req')), 'req', 0, 0)  288 us
    unnamed x19, local copies, waits for them, and re-layouts  32.1 us
    all_to_all x1, blocking collectives, body(): lax.all_to_all(halves.astype(jnp.bfloat16), 'guide', split_axis=0, concat...  23.7 us
    slice x1, local copies, waits for them, and re-layouts, masked_scores(): key_rows = page_rows[:, :, :half_width].reshape(count, span, KVH, HD)  16.9 us
    reduce_scatter x1, waiting for transfers between devices, body(): lax.psum_scatter(jnp.einsum('grc,cd->grd', selected, w_out, preferred_ele...  15.3 us
    gather x4, local copies, waits for them, and re-layouts, body(): pages_sent = pool[tables[held_request, :MIGP]]  11.9 us
    gather x1, local copies, waits for them, and re-layouts, gather_pages(): picked = pool[tables]  11.3 us
  transfers between devices with their start and end apart: 8, of which 2 were waited for; matrix products, arithmetic and copies ran while one was open for 16% of the time, Pallas kernels for 0%

profile of v1, /device:TPU:32, one launch (start us, length us, event | category | flops | bytes accessed | tf_op | source)
XLA Modules:
  0.0 488.0 jit_solution(2344899492356520365)
XLA Ops:
  6.5 0.8 copy.45
  7.4 0.7 fusion.56
  9.5 0.6 fusion.55
  11.3 0.7 fusion.54
  13.3 0.7 fusion.53
  17.8 1.5 constant_dynamic-slice_fusion.8
  26.8 1.0 fusion.60
  27.9 2.6 gather_fusion
  30.5 1.9 collective-permute-start.1
  32.4 2.7 gather_fusion.1
  35.1 6.8 %collective-permute-start.2 = (bf16[2,64,640]{2,1,0:T(8,128)(2,1)S(1)}, bf16[2,64,640]{2,1,0:T(8,128)(2,1)S(1)}, u32[]{:S(2)}, u32[]{:S(2)}) collective-permute-start(bf16[2,64,640]{2,1,0:T(8,128)(2,1)S(1)} %gather_fusion.1), channel_id=1, source_target_pairs={{0,127},{1,0},{2,1},{3,2},{4,3},{5,4},{6,5},{7,6},{8,7},{9,8},{10,... | collective-permute-start | bytes 491528 | tf_op jit(solution)/shard_map/ppermute | solution.py:30
  41.9 3.3 gather_fusion.2
  45.2 3.3 gather_fusion.3
  48.5 1.0 fusion.21
  49.5 1.6 fusion.23
  51.1 2.7 collective-permute-start
  53.9 4.2 constant_dynamic-update-slice_fusion.4
  58.2 0.2 compare_reduce_fusion
  58.6 0.8 compare_select_fusion.1
  59.6 0.8 fusion.67
  60.4 3.7 fusion
  64.1 0.2 reduce-scatter.5.cloned.1.call-start
  64.4 0.7 constant_dynamic-update-slice_fusion.3
  65.1 0.7 constant_dynamic-update-slice_fusion.2
  65.8 1.6 constant_dynamic-update-slice_fusion.1
  67.4 1.6 constant_dynamic-update-slice_fusion
  69.0 11.3 %gather_fusion.4 = bf16[192,64,640]{2,1,0:T(8,128)(2,1)} fusion(bf16[54,64,640]{2,1,0:T(8,128)(2,1)} %constant_dynamic-update-slice_fusion, s32[1024]{0:T(1024)S(1)} %pad_clamp_fusion), kind=kCustom, calls=%fused_computation.4 | custom fusion | bytes 31458048 | tf_op jit(solution)/shard_map/gather | solution.py:69
  80.3 16.9 %fusion.71 = (bf16[24,512,320]{2,1,0:T(8,128)(2,1)}, bf16[24,512,320]{2,1,0:T(8,128)(2,1)}) fusion(bf16[24,512,640]{2,1,0:T(8,128)(2,1)} %bitcast.147), kind=kLoop, calls=%fused_computation.135 | loop fusion | bytes 31457280 | tf_op jit(solution)/shard_map/slice | solution.py:41
  97.2 11.6 %copy.27 = bf16[24,512,320]{1,2,0:T(8,128)(2,1)} copy(bf16[24,512,320]{2,1,0:T(8,128)(2,1)} %get-tuple-element.17) | data formatting | bytes 15728640
  108.7 11.5 %copy.28 = bf16[24,512,320]{1,2,0:T(8,128)(2,1)} copy(bf16[24,512,320]{2,1,0:T(8,128)(2,1)} %get-tuple-element.18) | data formatting | bytes 15728640
  120.2 0.9 convert_bitcast_fusion.2
  121.5 0.3 fusion.73
  121.8 4.5 fusion.72
  126.3 0.9 copy-done.1
  127.2 0.6 fusion.14
  127.9 5.8 %fusion.12 = bf16[24,5,4,64]{3,2,1,0:T(4,128)(2,1)S(1)} fusion(bf16[24,512,5,64]{1,3,2,0:T(8,128)(2,1)} %bitcast.150, f32[24,5,4,512]{3,2,1,0:T(4,128)} %copy-done.1, f32[24,5,4]{2,1,0:T(8,128)S(1)} %fusion.38, f32[24,5,4]{2,1,0:T(8,128)S(1)} %get-tuple-element.20, f32[24,5,64]{2,1,0:T(8,128)S(1)} %reshape.373, f32[24,5,4]{2,1,0:T(8,128)S(1)} %get-tuple-element.19), kind=kOutput, calls=%fused_computation.20 | convolution fusion | flops 32071680 | bytes 8945280 | tf_op jit(solution)/shard_map/rkgs,rskd->rkgd/dot_general | solution.py:57
  133.9 0.8 collective-permute-start.5
  134.8 4.9 %collective-permute-done.5 = bf16[24,1280]{1,0:T(8,128)(2,1)S(1)} collective-permute-done((bf16[24,1280]{1,0:T(8,128)(2,1)S(1)}, bf16[24,1280]{1,0:T(8,128)(2,1)S(1)}, u32[]{:S(2)}, u32[]{:S(2)}) %collective-permute-start.5) | collective-permute-done | bytes 61472 | tf_op jit(solution)/shard_map/ppermute | solution.py:24
  139.7 1.2 fusion.4
  141.0 15.3 %reduce-scatter.5.cloned.1.call-done = bf16[1,24,2048]{2,1,0:T(8,128)(2,1)} async-done(((bf16[2,24,2048]{2,1,0:T(8,128)(2,1)}), bf16[1,24,2048]{2,1,0:T(8,128)(2,1)}) %reduce-scatter.5.cloned.1.call-update) | async-done | bytes 98320 | tf_op jit(solution)/shard_map/reduce_scatter | solution.py:156
  156.2 1.0 fusion.25
  157.3 1.0 fusion.36
  158.3 6.2 %stack.23 = bf16[128,24,2048]{2,1,0:T(8,128)(2,1)} broadcast(bf16[24,2048]{1,0:T(8,128)(2,1)S(1)} %fusion.36), dimensions={1,2} | broadcast | bytes 12681216 | tf_op jit(solution)/shard_map/stack | solution.py:168
  164.4 287.8 %all_to_all.10 = bf16[128,24,2048]{2,1,0:T(8,128)(2,1)S(1)} all-to-all(bf16[128,24,2048]{2,1,0:T(8,128)(2,1)} %stack.23), channel_id=1, replica_groups=mesh['guide'=2,'req'=128] {'req'}, dimensions={0} | all-to-all | bytes 25165824 | tf_op jit(solution)/shard_map/all_to_all | solution.py:168
  452.3 3.6 convolution_convert_fusion
  455.9 23.7 %all_to_all.11 = bf16[2,1536,250]{2,1,0:T(8,128)(2,1)S(1)} all-to-all(bf16[2,1536,250]{2,1,0:T(8,128)(2,1)S(1)} %convolution_convert_fusion), channel_id=1, replica_groups=mesh['guide'=2,'req'=128] {'guide'}, dimensions={0} | all-to-all | bytes 3072000 | tf_op jit(solution)/shard_map/all_to_all | solution.py:174
  479.6 0.2 convert_element_type.92
  479.8 1.3 fusion.9
  (49 shorter events, 1.4 us)
Async XLA Ops:
  6.5 133.2 %copy-start = (bf16[640,2048]{1,0:T(8,128)(2,1)S(1)}, bf16[640,2048]{1,0:T(8,128)(2,1)}, u32[]{:S(2)}) copy-start(bf16[640,2048]{1,0:T(8,128)(2,1)} %param.13) | copy-start | bytes 7864324
  6.5 113.7 %reduce-scatter.7.cloned.1.call-start = ((), (), s32[]{:S(2)}) async-start(), calls=%async_computation.5 | async-start | bytes 552960
  30.5 33.9 %collective-permute-start.1 = (bf16[2,64,640]{2,1,0:T(8,128)(2,1)S(1)}, bf16[2,64,640]{2,1,0:T(8,128)(2,1)S(1)}, u32[]{:S(2)}, u32[]{:S(2)}) collective-permute-start(bf16[2,64,640]{2,1,0:T(8,128)(2,1)S(1)} %gather_fusion), channel_id=1, source_target_pairs={{0,126},{1,127},{2,0},{3,1},{4,2},{5,3},{6,4},{7,5},{8,6},{9,7},{1... | collective-permute-start | bytes 491528 | tf_op jit(solution)/shard_map/ppermute | solution.py:30
  32.4 25.7 %copy-start.2 = (bf16[1,24,2048]{2,1,0:T(8,128)(2,1)S(1)}, bf16[1,24,2048]{2,1,0:T(8,128)(2,1)}, u32[]{:S(2)}) copy-start(bf16[1,24,2048]{2,1,0:T(8,128)(2,1)} %param.10) | copy-start | bytes 294916
  32.4 25.7 %copy-start.3 = (f32[2048]{0:T(1024)S(1)}, f32[2048]{0:T(1024)}, u32[]{:S(2)}) copy-start(f32[2048]{0:T(1024)} %param.11) | copy-start | bytes 24580
  35.1 30.0 %collective-permute-start.2 = (bf16[2,64,640]{2,1,0:T(8,128)(2,1)S(1)}, bf16[2,64,640]{2,1,0:T(8,128)(2,1)S(1)}, u32[]{:S(2)}, u32[]{:S(2)}) collective-permute-start(bf16[2,64,640]{2,1,0:T(8,128)(2,1)S(1)} %gather_fusion.1), channel_id=1, source_target_pairs={{0,127},{1,0},{2,1},{3,2},{4,3},{5,4},{6,5},{7,6},{8,7},{9,8},{10,... | collective-permute-start | bytes 491528 | tf_op jit(solution)/shard_map/ppermute | solution.py:30
  45.2 20.6 %collective-permute-start.3 = (bf16[2,64,640]{2,1,0:T(8,128)(2,1)}, bf16[2,64,640]{2,1,0:T(8,128)(2,1)}, u32[]{:S(2)}, u32[]{:S(2)}) collective-permute-start(bf16[2,64,640]{2,1,0:T(8,128)(2,1)} %gather_fusion.2), channel_id=1, source_target_pairs={{0,1},{1,2},{2,3},{3,4},{4,5},{5,6},{6,7},{7,8},{8,9},{9,10},{10,1... | collective-permute-start | bytes 491528 | tf_op jit(solution)/shard_map/ppermute | solution.py:30
  48.5 18.9 %collective-permute-start.4 = (bf16[2,64,640]{2,1,0:T(8,128)(2,1)}, bf16[2,64,640]{2,1,0:T(8,128)(2,1)}, u32[]{:S(2)}, u32[]{:S(2)}) collective-permute-start(bf16[2,64,640]{2,1,0:T(8,128)(2,1)} %gather_fusion.3), channel_id=1, source_target_pairs={{0,2},{1,3},{2,4},{3,5},{4,6},{5,7},{6,8},{7,9},{8,10},{9,11},{10,... | collective-permute-start | bytes 491528 | tf_op jit(solution)/shard_map/ppermute | solution.py:30
  51.1 9.3 %collective-permute-start = (bf16[24,2048]{1,0:T(8,128)(2,1)}, bf16[24,2048]{1,0:T(8,128)(2,1)}, u32[]{:S(2)}, u32[]{:S(2)}) collective-permute-start(bf16[24,2048]{1,0:T(8,128)(2,1)} %fusion.23), channel_id=1, source_target_pairs={{0,128},{128,0},{1,129},{129,1},{2,130},{130,2},{3,131},{131,3},{4... | collective-permute-start | bytes 294920 | tf_op jit(solution)/shard_map/ppermute | solution.py:24
  64.1 92.1 %reduce-scatter.5.cloned.1.call-start = ((), (), s32[]{:S(2)}) async-start(), calls=%async_computation.4 | async-start | bytes 294912 | tf_op jit(solution)/shard_map/reduce_scatter | solution.py:156
  126.2 0.9 copy-start.1
  133.7 23.5 %copy-start.4 = (f32[2048]{0:T(1024)S(1)}, f32[2048]{0:T(1024)}, u32[]{:S(2)}) copy-start(f32[2048]{0:T(1024)} %param.14) | copy-start | bytes 24580
  133.9 5.8 %collective-permute-start.5 = (bf16[24,1280]{1,0:T(8,128)(2,1)S(1)}, bf16[24,1280]{1,0:T(8,128)(2,1)S(1)}, u32[]{:S(2)}, u32[]{:S(2)}) collective-permute-start(bf16[24,1280]{1,0:T(8,128)(2,1)S(1)} %convert_element_type.87), channel_id=1, source_target_pairs={{0,128},{128,0},{1,129},{129,1},{2,130},{130,2},{3,131},{131,3},{4... | collective-permute-start | bytes 184328 | tf_op jit(solution)/shard_map/ppermute | solution.py:24
  164.4 287.9 %copy-start.5 = (bf16[2048,250]{1,0:T(8,128)(2,1)S(1)}, bf16[2048,250]{1,0:T(8,128)(2,1)}, u32[]{:S(2)}) copy-start(bf16[2048,250]{1,0:T(8,128)(2,1)} %param.15) | copy-start | bytes 3072004
Sparse Core Ops, SparseCore 0:
  64.3 17.4 reduce-scatter.6
  141.1 15.0 reduce-scatter.4
